TPU v7x, 128 devices: a whole 4x4x4 slice. The times are simulated.
128 devices in a mesh: depth: 8 (over z, core), plane: 16 (over x, y).
Axes of the slice: x: 4, y: 4, z: 4, core: 2. Of those that a mesh axis runs over, the one named last changes fastest.
Arguments:
- toar: bfloat16 [8, 8, 2, 32768], P('depth', None, None, 'plane'), may hold values from -6 to 6
- pml_coeff: float32 [8, 2, 32768], P('depth', None, 'plane'), may hold values from -1.5 to 1.5
- coupling: float32 [8, 32768], P('depth', 'plane'), may hold values from 0.5 to 1
- inverse: bfloat16 [8, 512, 16, 64, 128], P('depth', 'plane'), may hold values from -0.125 to 0.125
- pattern: int32 [8, 512, 16], P('depth', 'plane'), may hold values from 0 to 511
- patch_map: int32 [8, 32768], P('depth', 'plane'), may hold values from 0 to 16383, as said below
Outputs:
- precond: bfloat16 [8, 8, 2, 32768], P('depth', None, None, 'plane')
- patch_sens: float32 [8, 16384], P(None, ('depth', 'plane'))
Inputs may be any that keep to these rules, and one draw needn't show every extreme that they name: `patch_map`: patch p belongs to owner p // 128. Among the cells of one device (one layer, one block of 2048 cells), at most 32 name patches of any one owner, and in every such block some owner is named exactly 32 times. `pattern`: block columns of the whole layer.
All inputs are finite; a program needn't handle non-finite values.
Results may differ from a plain program's by a relative error of at most 0.018.
Values may be sent and summed in bfloat16 or wider, within the bound.
No kernel may reach another device: no remote copies, remote signals or barrier semaphores. Data moves between devices by JAX's collectives and lax.ppermute only.
A program may use at most 128 MiB of HBM per device.

v0:
```python
import jax
import jax.numpy as jnp
from jax import lax
from jax.sharding import PartitionSpec as P

PATCH_DEV = 128
CAP = 32


def passed_along(value, axis, steps):
    count = lax.axis_size(axis)
    first, last = (max(0, -steps), min(count, count - steps))
    return lax.ppermute(value, axis, [(source, source + steps) for source in range(first, last)])


def shards(toar, pml_coeff, coupling, inverse, pattern, patch_map):
    toar_local = toar[0]
    coeff = pml_coeff[0]
    coupler = coupling[0]
    factor = inverse[0]
    pattern_flat = pattern[0].reshape(-1)
    block_rows = factor.shape[0]
    block_cells = factor.shape[2]
    depth_count = lax.axis_size("depth")
    plane_count = lax.axis_size("plane")
    vec_count = toar_local.shape[0]
    toar_f32 = toar_local.astype(jnp.float32)
    real_part = coeff[0] * toar_f32[:, 0] - coeff[1] * toar_f32[:, 1]
    imag_part = coeff[0] * toar_f32[:, 1] + coeff[1] * toar_f32[:, 0]
    source = jnp.stack([real_part, imag_part], axis=1)

    def apply_layer(incoming):
        local_blocks = incoming.reshape(vec_count, 2, block_rows, block_cells).transpose(2, 0, 1, 3)
        gathered = lax.all_gather(local_blocks, "plane", axis=0, tiled=True)
        chosen = jnp.take(gathered, pattern_flat, axis=0)
        chosen = chosen.reshape(block_rows, -1, vec_count, 2, block_cells)
        x_re = chosen[:, :, :, 0]
        x_im = chosen[:, :, :, 1]
        expanded = jnp.stack(
            [jnp.concatenate([x_re, -x_im], axis=-1), jnp.concatenate([x_im, x_re], axis=-1)],
            axis=3,
        )
        out = jnp.einsum("rkic,rkvwc->vwri", factor, expanded, preferred_element_type=jnp.float32)
        return out.reshape(vec_count, 2, block_rows * block_cells)

    def down_turn(turn_index, current):
        arrived = passed_along(current, "depth", 1)
        down_in = (source + coupler * arrived.astype(jnp.float32)).astype(jnp.bfloat16)
        return apply_layer(down_in).astype(jnp.bfloat16)

    first = apply_layer(source.astype(jnp.bfloat16)).astype(jnp.bfloat16)
    swept = lax.fori_loop(0, depth_count - 1, down_turn, first)

    def up_turn(turn_index, current):
        outgoing = (coupler * current.astype(jnp.float32)).astype(jnp.bfloat16)
        arrived = passed_along(outgoing, "depth", -1)
        return (swept.astype(jnp.float32) + apply_layer(arrived)).astype(jnp.bfloat16)

    precond = lax.fori_loop(0, depth_count - 1, up_turn, swept)
    product = precond.astype(jnp.float32) * toar_f32
    contrib = product[:, 0] + product[:, 1]
    cell_patch = patch_map[0]
    cell_count = cell_patch.shape[0]
    owner_count = depth_count * plane_count
    owner = cell_patch // PATCH_DEV
    hits = (owner[:, None] == jnp.arange(owner_count, dtype=owner.dtype)[None, :]).astype(jnp.int32)
    rank = jnp.take_along_axis(jnp.cumsum(hits, axis=0), owner[:, None], axis=1)[:, 0] - 1
    slot = owner * CAP + rank
    cells = jnp.arange(cell_count, dtype=jnp.int32)
    perm = jnp.full((owner_count * CAP,), cell_count, jnp.int32).at[slot].set(cells)
    local_patch = (cell_patch % PATCH_DEV).astype(jnp.float32)
    padded = jnp.concatenate(
        [
            jnp.concatenate([contrib.T, local_patch[:, None]], axis=1),
            jnp.zeros((1, vec_count + 1), jnp.float32),
        ],
        axis=0,
    )
    packed = jnp.take(padded, perm, axis=0).reshape(owner_count, CAP, vec_count + 1)
    received = lax.all_to_all(packed, ("depth", "plane"), 0, 0, tiled=True)
    received = received.reshape(owner_count * CAP, vec_count + 1)
    target = received[:, vec_count].astype(jnp.int32)
    owned = jax.ops.segment_sum(received[:, :vec_count], target, num_segments=PATCH_DEV).T
    return (precond[None], owned)


def solution(mesh):
    return jax.shard_map(
        shards,
        mesh=mesh,
        in_specs=(
            P("depth", None, None, "plane"),
            P("depth", None, "plane"),
            P("depth", "plane"),
            P("depth", "plane", None, None, None),
            P("depth", "plane", None),
            P("depth", "plane"),
        ),
        out_specs=(P("depth", None, None, "plane"), P(None, ("depth", "plane"))),
        check_vma=False,
    )
```

profile of v0, /device:TPU:1, one launch (start us, length us, event | category | flops | bytes accessed | tf_op | source)
XLA Modules:
  0.0 989.7 jit_solution(395873803658313803)
XLA Ops:
  13.6 16.8 %gather_fusion.3 = s32[2048]{0:T(1024)S(1)} fusion(s32[2048,128]{0,1:T(8,128)S(1)} %bitcast.223, s32[2048]{0:T(1024)S(1)} %bitcast.222), kind=kCustom, calls=%fused_computation.4 | custom fusion | bytes 32768 | tf_op jit(solution)/shard_map/jit(take_along_axis)/gather | solution.py:67
  30.5 8.2 scatter_custom_fusion
  39.0 18.4 %all-gather.4.cloned.1.call-done = bf16[512,8,2,64]{3,1,2,0:T(8,128)(2,1)} async-done(((bf16[32,8,2,64]{3,1,2,0:T(8,128)(2,1)}), bf16[512,8,2,64]{3,1,2,0:T(8,128)(2,1)}) %all-gather.4.cloned.1.call-update) | async-done | bytes 1048592 | tf_op jit(solution)/shard_map/all_gather | solution.py:34
  67.9 430.5 %while.20 = (s32[]{:T(128)}, bf16[8,2,2048]{2,0,1:T(8,128)(2,1)S(1)}, f32[1,2048]{1,0:T(1,128)S(1)}, f32[8,2,2048]{2,0,1:T(8,128)S(1)}, s32[512]{0:T(512)S(1)}, /*index=5*/bf16[32,16,64,128]{3,2,1,0:T(8,128)(2,1)}, s32[]{:T(128)}) while((s32[]{:T(128)}, bf16[8,2,2048]{2,0,1:T(8,128)(2,1)S(1)}, f32[1,2048]{1,0:T(1,128)S(1)}, ...), condition=%wide.region_1.3_spmd, body=%wide.region_0.0_spmd.sunk | while | flops 140416512 | bytes 54353100 | solution.py:52
  68.0 4.6 collective-permute-start
  74.8 44.0 %all-gather.6.cloned.1.call-done = bf16[512,8,2,64]{3,1,2,0:T(8,128)(2,1)} async-done(((bf16[32,8,2,64]{3,1,2,0:T(8,128)(2,1)}), bf16[512,8,2,64]{3,1,2,0:T(8,128)(2,1)}) %all-gather.6.cloned.1.call-update) | async-done | bytes 1048592 | tf_op jit(solution)/shard_map/while/body/eval_jaxpr/all_gather | solution.py:34
  136.3 44.0 %all-gather.6.cloned.1.call-done = bf16[512,8,2,64]{3,1,2,0:T(8,128)(2,1)} async-done(((bf16[32,8,2,64]{3,1,2,0:T(8,128)(2,1)}), bf16[512,8,2,64]{3,1,2,0:T(8,128)(2,1)}) %all-gather.6.cloned.1.call-update) | async-done | bytes 1048592 | tf_op jit(solution)/shard_map/while/body/eval_jaxpr/all_gather | solution.py:34
  197.8 44.0 %all-gather.6.cloned.1.call-done = bf16[512,8,2,64]{3,1,2,0:T(8,128)(2,1)} async-done(((bf16[32,8,2,64]{3,1,2,0:T(8,128)(2,1)}), bf16[512,8,2,64]{3,1,2,0:T(8,128)(2,1)}) %all-gather.6.cloned.1.call-update) | async-done | bytes 1048592 | tf_op jit(solution)/shard_map/while/body/eval_jaxpr/all_gather | solution.py:34
  259.3 44.0 %all-gather.6.cloned.1.call-done = bf16[512,8,2,64]{3,1,2,0:T(8,128)(2,1)} async-done(((bf16[32,8,2,64]{3,1,2,0:T(8,128)(2,1)}), bf16[512,8,2,64]{3,1,2,0:T(8,128)(2,1)}) %all-gather.6.cloned.1.call-update) | async-done | bytes 1048592 | tf_op jit(solution)/shard_map/while/body/eval_jaxpr/all_gather | solution.py:34
  320.8 44.0 %all-gather.6.cloned.1.call-done = bf16[512,8,2,64]{3,1,2,0:T(8,128)(2,1)} async-done(((bf16[32,8,2,64]{3,1,2,0:T(8,128)(2,1)}), bf16[512,8,2,64]{3,1,2,0:T(8,128)(2,1)}) %all-gather.6.cloned.1.call-update) | async-done | bytes 1048592 | tf_op jit(solution)/shard_map/while/body/eval_jaxpr/all_gather | solution.py:34
  382.4 44.0 %all-gather.6.cloned.1.call-done = bf16[512,8,2,64]{3,1,2,0:T(8,128)(2,1)} async-done(((bf16[32,8,2,64]{3,1,2,0:T(8,128)(2,1)}), bf16[512,8,2,64]{3,1,2,0:T(8,128)(2,1)}) %all-gather.6.cloned.1.call-update) | async-done | bytes 1048592 | tf_op jit(solution)/shard_map/while/body/eval_jaxpr/all_gather | solution.py:34
  443.9 44.0 %all-gather.6.cloned.1.call-done = bf16[512,8,2,64]{3,1,2,0:T(8,128)(2,1)} async-done(((bf16[32,8,2,64]{3,1,2,0:T(8,128)(2,1)}), bf16[512,8,2,64]{3,1,2,0:T(8,128)(2,1)}) %all-gather.6.cloned.1.call-update) | async-done | bytes 1048592 | tf_op jit(solution)/shard_map/while/body/eval_jaxpr/all_gather | solution.py:34
  498.4 425.7 %while.21 = (s32[]{:T(128)}, bf16[8,2,2048]{2,0,1:T(8,128)(2,1)S(1)}, bf16[8,2,2048]{2,0,1:T(8,128)(2,1)S(1)}, f32[1,2048]{1,0:T(1,128)S(1)}, s32[512]{0:T(512)S...) while((s32[]{:T(128)}, bf16[8,2,2048]{2,0,1:T(8,128)(2,1)S(1)}, bf16[8,2,2048]{2,0,1:T(8,128)(2,1)S(1)}, ...), condition=%wide.region_3.5_spmd, body=%wide.region_2.4_spmd.sunk | while | flops 140449280 | bytes 54811852 | solution.py:59
  506.2 42.7 %all-gather.8.cloned.1.call-done = bf16[512,8,2,64]{3,1,2,0:T(8,128)(2,1)} async-done(((bf16[32,8,2,64]{3,1,2,0:T(8,128)(2,1)}), bf16[512,8,2,64]{3,1,2,0:T(8,128)(2,1)}) %all-gather.8.cloned.1.call-update) | async-done | bytes 1048592 | tf_op jit(solution)/shard_map/while/body/eval_jaxpr/all_gather | solution.py:34
  567.0 42.7 %all-gather.8.cloned.1.call-done = bf16[512,8,2,64]{3,1,2,0:T(8,128)(2,1)} async-done(((bf16[32,8,2,64]{3,1,2,0:T(8,128)(2,1)}), bf16[512,8,2,64]{3,1,2,0:T(8,128)(2,1)}) %all-gather.8.cloned.1.call-update) | async-done | bytes 1048592 | tf_op jit(solution)/shard_map/while/body/eval_jaxpr/all_gather | solution.py:34
  627.8 42.7 %all-gather.8.cloned.1.call-done = bf16[512,8,2,64]{3,1,2,0:T(8,128)(2,1)} async-done(((bf16[32,8,2,64]{3,1,2,0:T(8,128)(2,1)}), bf16[512,8,2,64]{3,1,2,0:T(8,128)(2,1)}) %all-gather.8.cloned.1.call-update) | async-done | bytes 1048592 | tf_op jit(solution)/shard_map/while/body/eval_jaxpr/all_gather | solution.py:34
  688.6 42.7 %all-gather.8.cloned.1.call-done = bf16[512,8,2,64]{3,1,2,0:T(8,128)(2,1)} async-done(((bf16[32,8,2,64]{3,1,2,0:T(8,128)(2,1)}), bf16[512,8,2,64]{3,1,2,0:T(8,128)(2,1)}) %all-gather.8.cloned.1.call-update) | async-done | bytes 1048592 | tf_op jit(solution)/shard_map/while/body/eval_jaxpr/all_gather | solution.py:34
  749.4 42.7 %all-gather.8.cloned.1.call-done = bf16[512,8,2,64]{3,1,2,0:T(8,128)(2,1)} async-done(((bf16[32,8,2,64]{3,1,2,0:T(8,128)(2,1)}), bf16[512,8,2,64]{3,1,2,0:T(8,128)(2,1)}) %all-gather.8.cloned.1.call-update) | async-done | bytes 1048592 | tf_op jit(solution)/shard_map/while/body/eval_jaxpr/all_gather | solution.py:34
  810.1 42.7 %all-gather.8.cloned.1.call-done = bf16[512,8,2,64]{3,1,2,0:T(8,128)(2,1)} async-done(((bf16[32,8,2,64]{3,1,2,0:T(8,128)(2,1)}), bf16[512,8,2,64]{3,1,2,0:T(8,128)(2,1)}) %all-gather.8.cloned.1.call-update) | async-done | bytes 1048592 | tf_op jit(solution)/shard_map/while/body/eval_jaxpr/all_gather | solution.py:34
  870.9 42.7 %all-gather.8.cloned.1.call-done = bf16[512,8,2,64]{3,1,2,0:T(8,128)(2,1)} async-done(((bf16[32,8,2,64]{3,1,2,0:T(8,128)(2,1)}), bf16[512,8,2,64]{3,1,2,0:T(8,128)(2,1)}) %all-gather.8.cloned.1.call-update) | async-done | bytes 1048592 | tf_op jit(solution)/shard_map/while/body/eval_jaxpr/all_gather | solution.py:34
  924.7 10.8 %gather_fusion.2 = f32[4096,9]{1,0:T(8,128)S(1)} fusion(f32[2049,9]{1,0:T(8,128)S(1)} %concatenate.29, s32[4096]{0:T(1024)S(1)} %fusion.60), kind=kCustom, calls=%fused_computation.3 | custom fusion | bytes 311296 | tf_op jit(solution)/shard_map/jit(_take)/gather | solution.py:79
  937.6 8.5 all-to-all-start
  946.8 9.9 all-to-all-done
  959.7 22.8 %scatter_custom_fusion.1 = f32[128,8]{1,0:T(8,128)S(1)} fusion(s32[4096]{0:T(1024)S(1)} %bitcast.239, f32[4096,8]{1,0:T(8,128)S(1)} %copy.101, f32[]{:T(128)} %constant.77.clone.1), kind=kCustom, calls=%fused_computation.77 | custom fusion | flops 32768 | bytes 4100 | tf_op jit(solution)/shard_map/scatter-add | solution.py:83
  (414 shorter events, 266.7 us)
Async XLA Ops:
  7.2 50.2 %all-gather.4.cloned.1.call-start = ((), (), s32[]{:S(2)}) async-start(), calls=%async_computation.1 | async-start | bytes 2228224 | tf_op jit(solution)/shard_map/all_gather | solution.py:34
  67.9 50.9 %all-gather.6.cloned.1.call-start = ((), (), s32[]{:S(2)}) async-start(), calls=%async_computation.2 | async-start | bytes 2228224 | tf_op jit(solution)/shard_map/while/body/eval_jaxpr/all_gather | solution.py:34
  68.0 5.9 collective-permute-start
  129.4 50.9 %all-gather.6.cloned.1.call-start = ((), (), s32[]{:S(2)}) async-start(), calls=%async_computation.2 | async-start | bytes 2228224 | tf_op jit(solution)/shard_map/while/body/eval_jaxpr/all_gather | solution.py:34
  190.9 50.9 %all-gather.6.cloned.1.call-start = ((), (), s32[]{:S(2)}) async-start(), calls=%async_computation.2 | async-start | bytes 2228224 | tf_op jit(solution)/shard_map/while/body/eval_jaxpr/all_gather | solution.py:34
  252.4 50.9 %all-gather.6.cloned.1.call-start = ((), (), s32[]{:S(2)}) async-start(), calls=%async_computation.2 | async-start | bytes 2228224 | tf_op jit(solution)/shard_map/while/body/eval_jaxpr/all_gather | solution.py:34
  313.9 50.9 %all-gather.6.cloned.1.call-start = ((), (), s32[]{:S(2)}) async-start(), calls=%async_computation.2 | async-start | bytes 2228224 | tf_op jit(solution)/shard_map/while/body/eval_jaxpr/all_gather | solution.py:34
  375.4 50.9 %all-gather.6.cloned.1.call-start = ((), (), s32[]{:S(2)}) async-start(), calls=%async_computation.2 | async-start | bytes 2228224 | tf_op jit(solution)/shard_map/while/body/eval_jaxpr/all_gather | solution.py:34
  436.9 50.9 %all-gather.6.cloned.1.call-start = ((), (), s32[]{:S(2)}) async-start(), calls=%async_computation.2 | async-start | bytes 2228224 | tf_op jit(solution)/shard_map/while/body/eval_jaxpr/all_gather | solution.py:34
  498.7 50.2 %all-gather.8.cloned.1.call-start = ((), (), s32[]{:S(2)}) async-start(), calls=%async_computation.3 | async-start | bytes 2228224 | tf_op jit(solution)/shard_map/while/body/eval_jaxpr/all_gather | solution.py:34
  498.8 6.5 collective-permute-start.1
  559.5 50.2 %all-gather.8.cloned.1.call-start = ((), (), s32[]{:S(2)}) async-start(), calls=%async_computation.3 | async-start | bytes 2228224 | tf_op jit(solution)/shard_map/while/body/eval_jaxpr/all_gather | solution.py:34
  559.5 6.5 collective-permute-start.1
  620.2 50.2 %all-gather.8.cloned.1.call-start = ((), (), s32[]{:S(2)}) async-start(), calls=%async_computation.3 | async-start | bytes 2228224 | tf_op jit(solution)/shard_map/while/body/eval_jaxpr/all_gather | solution.py:34
  620.3 6.5 collective-permute-start.1
  681.0 50.2 %all-gather.8.cloned.1.call-start = ((), (), s32[]{:S(2)}) async-start(), calls=%async_computation.3 | async-start | bytes 2228224 | tf_op jit(solution)/shard_map/while/body/eval_jaxpr/all_gather | solution.py:34
  681.1 6.5 collective-permute-start.1
  741.8 50.2 %all-gather.8.cloned.1.call-start = ((), (), s32[]{:S(2)}) async-start(), calls=%async_computation.3 | async-start | bytes 2228224 | tf_op jit(solution)/shard_map/while/body/eval_jaxpr/all_gather | solution.py:34
  741.9 6.5 collective-permute-start.1
  802.6 50.2 %all-gather.8.cloned.1.call-start = ((), (), s32[]{:S(2)}) async-start(), calls=%async_computation.3 | async-start | bytes 2228224 | tf_op jit(solution)/shard_map/while/body/eval_jaxpr/all_gather | solution.py:34
  802.7 6.5 collective-permute-start.1
  863.4 50.2 %all-gather.8.cloned.1.call-start = ((), (), s32[]{:S(2)}) async-start(), calls=%async_computation.3 | async-start | bytes 2228224 | tf_op jit(solution)/shard_map/while/body/eval_jaxpr/all_gather | solution.py:34
  863.5 6.5 collective-permute-start.1
  937.6 19.1 %all-to-all-start = ((f32[128,1,288]{2,1,0:T(1,128)}), f32[128,1,288]{2,1,0:T(1,128)S(1)}, u32[]{:S(2)}, u32[]{:S(2)}) async-start(f32[128,1,288]{2,1,0:T(1,128)} %reshape.447), calls=%async_computation | async-start | bytes 393216 | tf_op jit(solution)/shard_map/all_to_all | solution.py:80
  (39 other events, 563.5 us)
Sparse Core Ops, SparseCore 0:
  10.1 47.1 all-gather.3
  74.9 43.8 all-gather.5
  136.4 43.8 all-gather.5
  197.9 43.8 all-gather.5
  259.4 43.8 all-gather.5
  320.9 43.8 all-gather.5
  382.4 43.8 all-gather.5
  443.9 43.8 all-gather.5
  506.3 42.5 all-gather.7
  567.1 42.5 all-gather.7
  627.9 42.5 all-gather.7
  688.7 42.5 all-gather.7
  749.4 42.5 all-gather.7
  810.2 42.5 all-gather.7
  871.0 42.5 all-gather.7
where the time goes:
time: 991 us; the launch traced here: 990 us
  waiting for transfers between devices  666 us (67%)
  local copies, waits for them, and re-layouts  134 us (14%)
  other arithmetic  73.8 us (7%)
  starting transfers between devices  65 us (7%)
  matrix products  34 us (3%)
  between operations  14.1 us (1%)
    all_gather x15, waiting for transfers between devices, apply_layer(): gathered = lax.all_gather(local_blocks, 'plane', axis=0, tiled=True)  625 us
    ppermute x14, starting transfers between devices, passed_along(): lax.ppermute(value, axis, [(source, source + steps) for source in range(f...  55.9 us
    gather x15, local copies, waits for them, and re-layouts, apply_layer(): chosen = jnp.take(gathered, pattern_flat, axis=0)  41.6 us
    dot_general x15, matrix products, apply_layer(): jnp.einsum('rkic,rkvwc->vwri', factor, expanded, preferred_element_type=j...  34 us
    ppermute x14, waiting for transfers between devices, passed_along(): lax.ppermute(value, axis, [(source, source + steps) for source in range(f...  30.8 us
    select_n x30, other arithmetic, apply_layer(): chosen = jnp.take(gathered, pattern_flat, axis=0)  26.4 us
    while x56, local copies, waits for them, and re-layouts  24.8 us
    scatter-add x1, other arithmetic, shards(): jax.ops.segment_sum(received[:, :vec_count], target, num_segments=PATCH_DEV)  22.8 us
  transfers between devices with their start and end apart: 30, of which 30 were waited for; matrix products, arithmetic and copies ran while one was open for 3% of the time, Pallas kernels for 0%

commit v1 on v0

--- a/solution.py
+++ b/solution.py
@@ -31,7 +31,10 @@
 
     def apply_layer(incoming):
         local_blocks = incoming.reshape(vec_count, 2, block_rows, block_cells).transpose(2, 0, 1, 3)
-        gathered = lax.all_gather(local_blocks, "plane", axis=0, tiled=True)
+        gathered = jnp.concatenate(
+            lax.all_to_all(jnp.stack([local_blocks] * lax.axis_size("plane")), "plane", 0, 0),
+            axis=0,
+        )
         chosen = jnp.take(gathered, pattern_flat, axis=0)
         chosen = chosen.reshape(block_rows, -1, vec_count, 2, block_cells)
         x_re = chosen[:, :, :, 0]

time: 991 us -> 707 us (0.71)
  waiting for transfers between devices: 666 us -> 265 us
  starting transfers between devices: 65 us -> 131 us
  local copies, waits for them, and re-layouts: 134 us -> 199 us
  between operations: 14.1 us -> 1.08 us
    all_gather x15 -> x0, waiting for transfers between devices: 625 us -> none  [apply_layer(): gathered = lax.all_gather(local_blocks, 'plane', axis=0, tiled=True)]
    all_to_all x0 -> x15, waiting for transfers between devices: none -> 192 us  [apply_layer(): lax.all_to_all(jnp.stack([local_blocks] * lax.axis_size('plane')), 'plane...]
    while x56 -> x98, local copies, waits for them, and re-layouts: 24.8 us -> 94.6 us
    all_to_all x0 -> x15, starting transfers between devices: none -> 59.7 us  [apply_layer(): lax.all_to_all(jnp.stack([local_blocks] * lax.axis_size('plane')), 'plane...]
    ppermute x14, waiting for transfers between devices: 30.8 us -> 63.2 us  [passed_along(): lax.ppermute(value, axis, [(source, source + steps) for source in range(f...]
    transpose x15, local copies, waits for them, and re-layouts: 10.8 us -> 0.85 us  [apply_layer(): incoming.reshape(vec_count, 2, block_rows, block_cells)]
  transfers between devices with their start and end apart: 30 -> 30, of which waited for: 30 -> 30; matrix products, arithmetic and copies ran while one was open for 3% -> 0% of each run, Pallas kernels for 0% -> 0%
where the time goes in v1:
time: 707 us; the launch traced here: 705 us
  waiting for transfers between devices  265 us (37%)
  local copies, waits for them, and re-layouts  199 us (28%)
  starting transfers between devices  131 us (19%)
  other arithmetic  72.1 us (10%)
  matrix products  34 us (5%)
    all_to_all x15, waiting for transfers between devices, apply_layer(): lax.all_to_all(jnp.stack([local_blocks] * lax.axis_size('plane')), 'plane...  192 us
    while x98, local copies, waits for them, and re-layouts  94.6 us
    ppermute x14, waiting for transfers between devices, passed_along(): lax.ppermute(value, axis, [(source, source + steps) for source in range(f...  63.2 us
    ppermute x14, starting transfers between devices, passed_along(): lax.ppermute(value, axis, [(source, source + steps) for source in range(f...  62.4 us
    all_to_all x15, starting transfers between devices, apply_layer(): lax.all_to_all(jnp.stack([local_blocks] * lax.axis_size('plane')), 'plane...  59.7 us
    gather x15, local copies, waits for them, and re-layouts, apply_layer(): chosen = jnp.take(gathered, pattern_flat, axis=0)  41.6 us
    dot_general x15, matrix products, apply_layer(): jnp.einsum('rkic,rkvwc->vwri', factor, expanded, preferred_element_type=j...  34 us
    select_n x30, other arithmetic, apply_layer(): chosen = jnp.take(gathered, pattern_flat, axis=0)  26.4 us
  transfers between devices with their start and end apart: 30, of which 30 were waited for; matrix products, arithmetic and copies ran while one was open for 0% of the time, Pallas kernels for 0%

profile of v1, /device:TPU:1, one launch (start us, length us, event | category | flops | bytes accessed | tf_op | source)
XLA Modules:
  0.0 704.7 jit_solution(11401269568389213457)
XLA Ops:
  7.0 16.8 %gather_fusion.3 = s32[2048]{0:T(1024)S(1)} fusion(s32[2048,128]{0,1:T(8,128)S(1)} %bitcast.249, s32[2048]{0:T(1024)S(1)} %bitcast.248), kind=kCustom, calls=%fused_computation.4 | custom fusion | bytes 32768 | tf_op jit(solution)/shard_map/jit(take_along_axis)/gather | solution.py:70
  40.4 15.4 %all-to-all-done.2 = bf16[16,2,16384]{2,1,0:T(2,128)(2,1)S(1)} async-done(((bf16[16,2,16384]{2,1,0:T(2,128)(2,1)}), bf16[16,2,16384]{2,1,0:T(2,128)(2,1)S(1)}, u32[]{:S(2)}, u32[]{:S(2)}) %all-to-all-start.2) | async-done | bytes 1048608 | tf_op jit(solution)/shard_map/all_to_all | solution.py:35
  68.7 286.7 %while.20 = (s32[]{:T(128)}, bf16[8,2,2048]{2,0,1:T(8,128)(2,1)S(1)}, f32[1,2048]{1,0:T(1,128)S(1)}, f32[8,2,2048]{2,0,1:T(8,128)S(1)}, s32[512]{0:T(512)S(1)}, /*index=5*/bf16[32,16,64,128]{3,2,1,0:T(8,128)(2,1)}, s32[]{:T(128)}) while((s32[]{:T(128)}, bf16[8,2,2048]{2,0,1:T(8,128)(2,1)S(1)}, f32[1,2048]{1,0:T(1,128)S(1)}, ...), condition=%wide.region_1.3_spmd, body=%wide.region_0.0_spmd.sunk | while | flops 140416512 | bytes 58350788 | solution.py:55
  83.2 15.4 %all-to-all-done = bf16[16,2,16384]{2,1,0:T(2,128)(2,1)S(1)} async-done(((bf16[16,2,16384]{2,1,0:T(2,128)(2,1)}), bf16[16,2,16384]{2,1,0:T(2,128)(2,1)S(1)}, u32[]{:S(2)}, u32[]{:S(2)}) %all-to-all-start) | async-done | bytes 1048608 | tf_op jit(solution)/shard_map/while/body/eval_jaxpr/all_to_all | solution.py:35
  126.1 13.1 %all-to-all-done = bf16[16,2,16384]{2,1,0:T(2,128)(2,1)S(1)} async-done(((bf16[16,2,16384]{2,1,0:T(2,128)(2,1)}), bf16[16,2,16384]{2,1,0:T(2,128)(2,1)S(1)}, u32[]{:S(2)}, u32[]{:S(2)}) %all-to-all-start) | async-done | bytes 1048608 | tf_op jit(solution)/shard_map/while/body/eval_jaxpr/all_to_all | solution.py:35
  168.2 11.8 %all-to-all-done = bf16[16,2,16384]{2,1,0:T(2,128)(2,1)S(1)} async-done(((bf16[16,2,16384]{2,1,0:T(2,128)(2,1)}), bf16[16,2,16384]{2,1,0:T(2,128)(2,1)S(1)}, u32[]{:S(2)}, u32[]{:S(2)}) %all-to-all-start) | async-done | bytes 1048608 | tf_op jit(solution)/shard_map/while/body/eval_jaxpr/all_to_all | solution.py:35
  208.4 12.3 %all-to-all-done = bf16[16,2,16384]{2,1,0:T(2,128)(2,1)S(1)} async-done(((bf16[16,2,16384]{2,1,0:T(2,128)(2,1)}), bf16[16,2,16384]{2,1,0:T(2,128)(2,1)S(1)}, u32[]{:S(2)}, u32[]{:S(2)}) %all-to-all-start) | async-done | bytes 1048608 | tf_op jit(solution)/shard_map/while/body/eval_jaxpr/all_to_all | solution.py:35
  248.6 12.7 %all-to-all-done = bf16[16,2,16384]{2,1,0:T(2,128)(2,1)S(1)} async-done(((bf16[16,2,16384]{2,1,0:T(2,128)(2,1)}), bf16[16,2,16384]{2,1,0:T(2,128)(2,1)S(1)}, u32[]{:S(2)}, u32[]{:S(2)}) %all-to-all-start) | async-done | bytes 1048608 | tf_op jit(solution)/shard_map/while/body/eval_jaxpr/all_to_all | solution.py:35
  288.7 13.1 %all-to-all-done = bf16[16,2,16384]{2,1,0:T(2,128)(2,1)S(1)} async-done(((bf16[16,2,16384]{2,1,0:T(2,128)(2,1)}), bf16[16,2,16384]{2,1,0:T(2,128)(2,1)S(1)}, u32[]{:S(2)}, u32[]{:S(2)}) %all-to-all-start) | async-done | bytes 1048608 | tf_op jit(solution)/shard_map/while/body/eval_jaxpr/all_to_all | solution.py:35
  328.9 13.7 %all-to-all-done = bf16[16,2,16384]{2,1,0:T(2,128)(2,1)S(1)} async-done(((bf16[16,2,16384]{2,1,0:T(2,128)(2,1)}), bf16[16,2,16384]{2,1,0:T(2,128)(2,1)S(1)}, u32[]{:S(2)}, u32[]{:S(2)}) %all-to-all-start) | async-done | bytes 1048608 | tf_op jit(solution)/shard_map/while/body/eval_jaxpr/all_to_all | solution.py:35
  355.4 289.5 %while.21 = (s32[]{:T(128)}, bf16[8,2,2048]{2,0,1:T(8,128)(2,1)S(1)}, bf16[8,2,2048]{2,0,1:T(8,128)(2,1)S(1)}, f32[1,2048]{1,0:T(1,128)S(1)}, s32[512]{0:T(512)S...) while((s32[]{:T(128)}, bf16[8,2,2048]{2,0,1:T(8,128)(2,1)S(1)}, bf16[8,2,2048]{2,0,1:T(8,128)(2,1)S(1)}, ...), condition=%wide.region_3.5_spmd, body=%wide.region_2.4_spmd.sunk | while | flops 140449280 | bytes 58809540 | solution.py:62
  369.9 13.3 %all-to-all-done.1 = bf16[16,2,16384]{2,1,0:T(2,128)(2,1)S(1)} async-done(((bf16[16,2,16384]{2,1,0:T(2,128)(2,1)}), bf16[16,2,16384]{2,1,0:T(2,128)(2,1)S(1)}, u32[]{:S(2)}, u32[]{:S(2)}) %all-to-all-start.1) | async-done | bytes 1048608 | tf_op jit(solution)/shard_map/while/body/eval_jaxpr/all_to_all | solution.py:35
  411.3 12.5 %all-to-all-done.1 = bf16[16,2,16384]{2,1,0:T(2,128)(2,1)S(1)} async-done(((bf16[16,2,16384]{2,1,0:T(2,128)(2,1)}), bf16[16,2,16384]{2,1,0:T(2,128)(2,1)S(1)}, u32[]{:S(2)}, u32[]{:S(2)}) %all-to-all-start.1) | async-done | bytes 1048608 | tf_op jit(solution)/shard_map/while/body/eval_jaxpr/all_to_all | solution.py:35
  452.9 11.7 %all-to-all-done.1 = bf16[16,2,16384]{2,1,0:T(2,128)(2,1)S(1)} async-done(((bf16[16,2,16384]{2,1,0:T(2,128)(2,1)}), bf16[16,2,16384]{2,1,0:T(2,128)(2,1)S(1)}, u32[]{:S(2)}, u32[]{:S(2)}) %all-to-all-start.1) | async-done | bytes 1048608 | tf_op jit(solution)/shard_map/while/body/eval_jaxpr/all_to_all | solution.py:35
  479.4 9.0 %collective-permute-done.1 = bf16[8,2,2048]{2,0,1:T(8,128)(2,1)S(1)} collective-permute-done((bf16[8,2,2048]{2,0,1:T(8,128)(2,1)S(1)}, bf16[8,2,2048]{2,0,1:T(8,128)(2,1)S(1)}, u32[]{:S(2)}, u32[]{:S(2)}) %collective-permute-start.1) | collective-permute-done | bytes 65568 | tf_op jit(solution)/shard_map/while/body/eval_jaxpr/ppermute | solution.py:13
  495.0 11.7 %all-to-all-done.1 = bf16[16,2,16384]{2,1,0:T(2,128)(2,1)S(1)} async-done(((bf16[16,2,16384]{2,1,0:T(2,128)(2,1)}), bf16[16,2,16384]{2,1,0:T(2,128)(2,1)S(1)}, u32[]{:S(2)}, u32[]{:S(2)}) %all-to-all-start.1) | async-done | bytes 1048608 | tf_op jit(solution)/shard_map/while/body/eval_jaxpr/all_to_all | solution.py:35
  521.5 9.8 %collective-permute-done.1 = bf16[8,2,2048]{2,0,1:T(8,128)(2,1)S(1)} collective-permute-done((bf16[8,2,2048]{2,0,1:T(8,128)(2,1)S(1)}, bf16[8,2,2048]{2,0,1:T(8,128)(2,1)S(1)}, u32[]{:S(2)}, u32[]{:S(2)}) %collective-permute-start.1) | collective-permute-done | bytes 65568 | tf_op jit(solution)/shard_map/while/body/eval_jaxpr/ppermute | solution.py:13
  537.9 11.7 %all-to-all-done.1 = bf16[16,2,16384]{2,1,0:T(2,128)(2,1)S(1)} async-done(((bf16[16,2,16384]{2,1,0:T(2,128)(2,1)}), bf16[16,2,16384]{2,1,0:T(2,128)(2,1)S(1)}, u32[]{:S(2)}, u32[]{:S(2)}) %all-to-all-start.1) | async-done | bytes 1048608 | tf_op jit(solution)/shard_map/while/body/eval_jaxpr/all_to_all | solution.py:35
  579.3 11.7 %all-to-all-done.1 = bf16[16,2,16384]{2,1,0:T(2,128)(2,1)S(1)} async-done(((bf16[16,2,16384]{2,1,0:T(2,128)(2,1)}), bf16[16,2,16384]{2,1,0:T(2,128)(2,1)S(1)}, u32[]{:S(2)}, u32[]{:S(2)}) %all-to-all-start.1) | async-done | bytes 1048608 | tf_op jit(solution)/shard_map/while/body/eval_jaxpr/all_to_all | solution.py:35
  620.3 11.7 %all-to-all-done.1 = bf16[16,2,16384]{2,1,0:T(2,128)(2,1)S(1)} async-done(((bf16[16,2,16384]{2,1,0:T(2,128)(2,1)}), bf16[16,2,16384]{2,1,0:T(2,128)(2,1)S(1)}, u32[]{:S(2)}, u32[]{:S(2)}) %all-to-all-start.1) | async-done | bytes 1048608 | tf_op jit(solution)/shard_map/while/body/eval_jaxpr/all_to_all | solution.py:35
  645.4 10.8 %gather_fusion.2 = f32[4096,9]{1,0:T(8,128)S(1)} fusion(f32[2049,9]{1,0:T(8,128)S(1)} %concatenate.29, s32[4096]{0:T(1024)S(1)} %fusion.60), kind=kCustom, calls=%fused_computation.3 | custom fusion | bytes 311296 | tf_op jit(solution)/shard_map/jit(_take)/gather | solution.py:82
  658.4 9.3 %all-to-all-start.3 = ((f32[128,1,288]{2,1,0:T(1,128)}), f32[128,1,288]{2,1,0:T(1,128)S(1)}, u32[]{:S(2)}, u32[]{:S(2)}) async-start(f32[128,1,288]{2,1,0:T(1,128)} %reshape.469), calls=%async_computation.3 | async-start | bytes 393216 | tf_op jit(solution)/shard_map/all_to_all | solution.py:83
  668.4 9.9 %all-to-all-done.3 = f32[128,1,288]{2,1,0:T(1,128)S(1)} async-done(((f32[128,1,288]{2,1,0:T(1,128)}), f32[128,1,288]{2,1,0:T(1,128)S(1)}, u32[]{:S(2)}, u32[]{:S(2)}) %all-to-all-start.3) | async-done | bytes 147488 | tf_op jit(solution)/shard_map/all_to_all | solution.py:83
  681.2 22.8 %scatter_custom_fusion.1 = f32[128,8]{1,0:T(8,128)S(1)} fusion(s32[4096]{0:T(1024)S(1)} %bitcast.266, f32[4096,8]{1,0:T(8,128)S(1)} %copy.72, f32[]{:T(128)} %constant.77.clone.1), kind=kCustom, calls=%fused_computation.77 | custom fusion | flops 32768 | bytes 4100 | tf_op jit(solution)/shard_map/scatter-add | solution.py:86
  (448 shorter events, 421.2 us)
Async XLA Ops:
  32.7 23.1 %all-to-all-start.2 = ((bf16[16,2,16384]{2,1,0:T(2,128)(2,1)}), bf16[16,2,16384]{2,1,0:T(2,128)(2,1)S(1)}, u32[]{:S(2)}, u32[]{:S(2)}) async-start(bf16[16,2,16384]{2,1,0:T(2,128)(2,1)} %reshape.467), calls=%async_computation.2 | async-start | bytes 2097152 | tf_op jit(solution)/shard_map/all_to_all | solution.py:35
  79.5 19.1 %all-to-all-start = ((bf16[16,2,16384]{2,1,0:T(2,128)(2,1)}), bf16[16,2,16384]{2,1,0:T(2,128)(2,1)S(1)}, u32[]{:S(2)}, u32[]{:S(2)}) async-start(bf16[16,2,16384]{2,1,0:T(2,128)(2,1)} %reshape.485), calls=%async_computation | async-start | bytes 2097152 | tf_op jit(solution)/shard_map/while/body/eval_jaxpr/all_to_all | solution.py:35
  122.4 16.8 %all-to-all-start = ((bf16[16,2,16384]{2,1,0:T(2,128)(2,1)}), bf16[16,2,16384]{2,1,0:T(2,128)(2,1)S(1)}, u32[]{:S(2)}, u32[]{:S(2)}) async-start(bf16[16,2,16384]{2,1,0:T(2,128)(2,1)} %reshape.485), calls=%async_computation | async-start | bytes 2097152 | tf_op jit(solution)/shard_map/while/body/eval_jaxpr/all_to_all | solution.py:35
  152.0 9.6 %collective-permute-start = (bf16[8,2,2048]{2,0,1:T(8,128)(2,1)S(1)}, bf16[8,2,2048]{2,0,1:T(8,128)(2,1)S(1)}, u32[]{:S(2)}, u32[]{:S(2)}) collective-permute-start(bf16[8,2,2048]{2,0,1:T(8,128)(2,1)S(1)} %get-tuple-element.229), channel_id=1, source_target_pairs={{0,16},{16,32},{32,48},{48,64},{64,80},{80,96},{96,112},{1,17},{17... | collective-permute-start | bytes 196616 | tf_op jit(solution)/shard_map/while/body/eval_jaxpr/ppermute | solution.py:13
  164.5 15.5 %all-to-all-start = ((bf16[16,2,16384]{2,1,0:T(2,128)(2,1)}), bf16[16,2,16384]{2,1,0:T(2,128)(2,1)S(1)}, u32[]{:S(2)}, u32[]{:S(2)}) async-start(bf16[16,2,16384]{2,1,0:T(2,128)(2,1)} %reshape.485), calls=%async_computation | async-start | bytes 2097152 | tf_op jit(solution)/shard_map/while/body/eval_jaxpr/all_to_all | solution.py:35
  192.9 8.9 %collective-permute-start = (bf16[8,2,2048]{2,0,1:T(8,128)(2,1)S(1)}, bf16[8,2,2048]{2,0,1:T(8,128)(2,1)S(1)}, u32[]{:S(2)}, u32[]{:S(2)}) collective-permute-start(bf16[8,2,2048]{2,0,1:T(8,128)(2,1)S(1)} %get-tuple-element.229), channel_id=1, source_target_pairs={{0,16},{16,32},{32,48},{48,64},{64,80},{80,96},{96,112},{1,17},{17... | collective-permute-start | bytes 196616 | tf_op jit(solution)/shard_map/while/body/eval_jaxpr/ppermute | solution.py:13
  204.7 16.0 %all-to-all-start = ((bf16[16,2,16384]{2,1,0:T(2,128)(2,1)}), bf16[16,2,16384]{2,1,0:T(2,128)(2,1)S(1)}, u32[]{:S(2)}, u32[]{:S(2)}) async-start(bf16[16,2,16384]{2,1,0:T(2,128)(2,1)} %reshape.485), calls=%async_computation | async-start | bytes 2097152 | tf_op jit(solution)/shard_map/while/body/eval_jaxpr/all_to_all | solution.py:35
  244.9 16.4 %all-to-all-start = ((bf16[16,2,16384]{2,1,0:T(2,128)(2,1)}), bf16[16,2,16384]{2,1,0:T(2,128)(2,1)S(1)}, u32[]{:S(2)}, u32[]{:S(2)}) async-start(bf16[16,2,16384]{2,1,0:T(2,128)(2,1)} %reshape.485), calls=%async_computation | async-start | bytes 2097152 | tf_op jit(solution)/shard_map/while/body/eval_jaxpr/all_to_all | solution.py:35
  285.0 16.8 %all-to-all-start = ((bf16[16,2,16384]{2,1,0:T(2,128)(2,1)}), bf16[16,2,16384]{2,1,0:T(2,128)(2,1)S(1)}, u32[]{:S(2)}, u32[]{:S(2)}) async-start(bf16[16,2,16384]{2,1,0:T(2,128)(2,1)} %reshape.485), calls=%async_computation | async-start | bytes 2097152 | tf_op jit(solution)/shard_map/while/body/eval_jaxpr/all_to_all | solution.py:35
  325.2 17.4 %all-to-all-start = ((bf16[16,2,16384]{2,1,0:T(2,128)(2,1)}), bf16[16,2,16384]{2,1,0:T(2,128)(2,1)S(1)}, u32[]{:S(2)}, u32[]{:S(2)}) async-start(bf16[16,2,16384]{2,1,0:T(2,128)(2,1)} %reshape.485), calls=%async_computation | async-start | bytes 2097152 | tf_op jit(solution)/shard_map/while/body/eval_jaxpr/all_to_all | solution.py:35
  366.2 17.0 %all-to-all-start.1 = ((bf16[16,2,16384]{2,1,0:T(2,128)(2,1)}), bf16[16,2,16384]{2,1,0:T(2,128)(2,1)S(1)}, u32[]{:S(2)}, u32[]{:S(2)}) async-start(bf16[16,2,16384]{2,1,0:T(2,128)(2,1)} %reshape.490), calls=%async_computation.1 | async-start | bytes 2097152 | tf_op jit(solution)/shard_map/while/body/eval_jaxpr/all_to_all | solution.py:35
  396.1 8.6 %collective-permute-start.1 = (bf16[8,2,2048]{2,0,1:T(8,128)(2,1)S(1)}, bf16[8,2,2048]{2,0,1:T(8,128)(2,1)S(1)}, u32[]{:S(2)}, u32[]{:S(2)}) collective-permute-start(bf16[8,2,2048]{2,0,1:T(8,128)(2,1)S(1)} %multiply_convert_fusion.2), channel_id=1, source_target_pairs={{16,0},{32,16},{48,32},{64,48},{80,64},{96,80},{112,96},{17,1},{33... | collective-permute-start | bytes 196616 | tf_op jit(solution)/shard_map/while/body/eval_jaxpr/ppermute | solution.py:13
  407.6 16.2 %all-to-all-start.1 = ((bf16[16,2,16384]{2,1,0:T(2,128)(2,1)}), bf16[16,2,16384]{2,1,0:T(2,128)(2,1)S(1)}, u32[]{:S(2)}, u32[]{:S(2)}) async-start(bf16[16,2,16384]{2,1,0:T(2,128)(2,1)} %reshape.490), calls=%async_computation.1 | async-start | bytes 2097152 | tf_op jit(solution)/shard_map/while/body/eval_jaxpr/all_to_all | solution.py:35
  436.6 9.7 %collective-permute-start.1 = (bf16[8,2,2048]{2,0,1:T(8,128)(2,1)S(1)}, bf16[8,2,2048]{2,0,1:T(8,128)(2,1)S(1)}, u32[]{:S(2)}, u32[]{:S(2)}) collective-permute-start(bf16[8,2,2048]{2,0,1:T(8,128)(2,1)S(1)} %multiply_convert_fusion.2), channel_id=1, source_target_pairs={{16,0},{32,16},{48,32},{64,48},{80,64},{96,80},{112,96},{17,1},{33... | collective-permute-start | bytes 196616 | tf_op jit(solution)/shard_map/while/body/eval_jaxpr/ppermute | solution.py:13
  449.2 15.4 %all-to-all-start.1 = ((bf16[16,2,16384]{2,1,0:T(2,128)(2,1)}), bf16[16,2,16384]{2,1,0:T(2,128)(2,1)S(1)}, u32[]{:S(2)}, u32[]{:S(2)}) async-start(bf16[16,2,16384]{2,1,0:T(2,128)(2,1)} %reshape.490), calls=%async_computation.1 | async-start | bytes 2097152 | tf_op jit(solution)/shard_map/while/body/eval_jaxpr/all_to_all | solution.py:35
  477.5 10.9 %collective-permute-start.1 = (bf16[8,2,2048]{2,0,1:T(8,128)(2,1)S(1)}, bf16[8,2,2048]{2,0,1:T(8,128)(2,1)S(1)}, u32[]{:S(2)}, u32[]{:S(2)}) collective-permute-start(bf16[8,2,2048]{2,0,1:T(8,128)(2,1)S(1)} %multiply_convert_fusion.2), channel_id=1, source_target_pairs={{16,0},{32,16},{48,32},{64,48},{80,64},{96,80},{112,96},{17,1},{33... | collective-permute-start | bytes 196616 | tf_op jit(solution)/shard_map/while/body/eval_jaxpr/ppermute | solution.py:13
  491.3 15.4 %all-to-all-start.1 = ((bf16[16,2,16384]{2,1,0:T(2,128)(2,1)}), bf16[16,2,16384]{2,1,0:T(2,128)(2,1)S(1)}, u32[]{:S(2)}, u32[]{:S(2)}) async-start(bf16[16,2,16384]{2,1,0:T(2,128)(2,1)} %reshape.490), calls=%async_computation.1 | async-start | bytes 2097152 | tf_op jit(solution)/shard_map/while/body/eval_jaxpr/all_to_all | solution.py:35
  519.6 11.8 %collective-permute-start.1 = (bf16[8,2,2048]{2,0,1:T(8,128)(2,1)S(1)}, bf16[8,2,2048]{2,0,1:T(8,128)(2,1)S(1)}, u32[]{:S(2)}, u32[]{:S(2)}) collective-permute-start(bf16[8,2,2048]{2,0,1:T(8,128)(2,1)S(1)} %multiply_convert_fusion.2), channel_id=1, source_target_pairs={{16,0},{32,16},{48,32},{64,48},{80,64},{96,80},{112,96},{17,1},{33... | collective-permute-start | bytes 196616 | tf_op jit(solution)/shard_map/while/body/eval_jaxpr/ppermute | solution.py:13
  534.2 15.4 %all-to-all-start.1 = ((bf16[16,2,16384]{2,1,0:T(2,128)(2,1)}), bf16[16,2,16384]{2,1,0:T(2,128)(2,1)S(1)}, u32[]{:S(2)}, u32[]{:S(2)}) async-start(bf16[16,2,16384]{2,1,0:T(2,128)(2,1)} %reshape.490), calls=%async_computation.1 | async-start | bytes 2097152 | tf_op jit(solution)/shard_map/while/body/eval_jaxpr/all_to_all | solution.py:35
  562.5 10.0 %collective-permute-start.1 = (bf16[8,2,2048]{2,0,1:T(8,128)(2,1)S(1)}, bf16[8,2,2048]{2,0,1:T(8,128)(2,1)S(1)}, u32[]{:S(2)}, u32[]{:S(2)}) collective-permute-start(bf16[8,2,2048]{2,0,1:T(8,128)(2,1)S(1)} %multiply_convert_fusion.2), channel_id=1, source_target_pairs={{16,0},{32,16},{48,32},{64,48},{80,64},{96,80},{112,96},{17,1},{33... | collective-permute-start | bytes 196616 | tf_op jit(solution)/shard_map/while/body/eval_jaxpr/ppermute | solution.py:13
  575.4 15.5 %all-to-all-start.1 = ((bf16[16,2,16384]{2,1,0:T(2,128)(2,1)}), bf16[16,2,16384]{2,1,0:T(2,128)(2,1)S(1)}, u32[]{:S(2)}, u32[]{:S(2)}) async-start(bf16[16,2,16384]{2,1,0:T(2,128)(2,1)} %reshape.490), calls=%async_computation.1 | async-start | bytes 2097152 | tf_op jit(solution)/shard_map/while/body/eval_jaxpr/all_to_all | solution.py:35
  603.9 9.0 %collective-permute-start.1 = (bf16[8,2,2048]{2,0,1:T(8,128)(2,1)S(1)}, bf16[8,2,2048]{2,0,1:T(8,128)(2,1)S(1)}, u32[]{:S(2)}, u32[]{:S(2)}) collective-permute-start(bf16[8,2,2048]{2,0,1:T(8,128)(2,1)S(1)} %multiply_convert_fusion.2), channel_id=1, source_target_pairs={{16,0},{32,16},{48,32},{64,48},{80,64},{96,80},{112,96},{17,1},{33... | collective-permute-start | bytes 196616 | tf_op jit(solution)/shard_map/while/body/eval_jaxpr/ppermute | solution.py:13
  615.8 16.3 %all-to-all-start.1 = ((bf16[16,2,16384]{2,1,0:T(2,128)(2,1)}), bf16[16,2,16384]{2,1,0:T(2,128)(2,1)S(1)}, u32[]{:S(2)}, u32[]{:S(2)}) async-start(bf16[16,2,16384]{2,1,0:T(2,128)(2,1)} %reshape.490), calls=%async_computation.1 | async-start | bytes 2097152 | tf_op jit(solution)/shard_map/while/body/eval_jaxpr/all_to_all | solution.py:35
  658.4 19.9 %all-to-all-start.3 = ((f32[128,1,288]{2,1,0:T(1,128)}), f32[128,1,288]{2,1,0:T(1,128)S(1)}, u32[]{:S(2)}, u32[]{:S(2)}) async-start(f32[128,1,288]{2,1,0:T(1,128)} %reshape.469), calls=%async_computation.3 | async-start | bytes 393216 | tf_op jit(solution)/shard_map/all_to_all | solution.py:83
  (41 other events, 428.1 us)
